TPU v7x, 1024 devices: a whole 4x8x16 slice. The times are simulated.
1024 devices in a mesh: bra: 16 (over z), ket: 64 (over y, x, core).
Axes of the slice: x: 4, y: 8, z: 16, core: 2. Of those that a mesh axis runs over, the one named last changes fastest.
Arguments:
- integrals: float32 [3072, 512, 512], P(('bra', 'ket')), may hold values from -0.046875 to 0.046875
- tile_place: int32 [3072, 2], P(('bra', 'ket')), may hold values from -1 to 63, as said below
- amplitudes: float32 [256, 32768], P('bra', 'ket'), may hold values from -6 to 6
- denominators: float32 [256, 32768], P('ket', 'bra'), may hold values from 1 to 4
Outputs:
- new_amplitudes: float32 [256, 32768], P('ket', 'bra')
Inputs may be any that keep to these rules, and one draw needn't show every extreme that they name: `tile_place`: device d = b * 64 + k (b its bra index, k its ket index) holds slots d * 3 to (d + 1) * 3 - 1. They list the nonzero tiles of its region, block rows b * 4 to (b + 1) * 4 - 1 and block columns k * 1 to (k + 1) - 1, in row-major order, followed by slots holding -1 in both entries. Every tile appears at most once. In every draw some device has all 3 slots filled.
All inputs are finite; a program needn't handle non-finite values.
Results may differ from a plain program's by a relative error of at most 0.0003.
Values sent between devices are 32-bit elements; how exact they have to be, the bound alone decides.
No kernel may reach another device: no remote copies, remote signals or barrier semaphores. Data moves between devices by JAX's collectives and lax.ppermute only.
A program may use at most 32 MiB of HBM per device.

v0:
```python
import jax
import jax.numpy as jnp
from jax import lax
from jax.sharding import PartitionSpec as P


def tile_term(amp_block, tile_now):
    return lax.dot_general(
        amp_block,
        tile_now,
        (((1,), (1,)), ((), ())),
        precision=lax.Precision.HIGHEST,
        preferred_element_type=jnp.float32,
    )


def add_block(partial_value, tile_product, block_row, tile_width):
    offset = block_row * tile_width
    current = lax.dynamic_slice_in_dim(partial_value, offset, tile_width, 1)
    return lax.dynamic_update_slice_in_dim(partial_value, current + tile_product, offset, 1)


def per_device(integrals, tile_place, amplitudes, denominators):
    tile_width = integrals.shape[1]
    row_blocks = denominators.shape[1] // tile_width
    local_rows = tile_place[:, 0] - lax.axis_index("bra") * row_blocks
    live_count = jnp.sum((tile_place[:, 0] >= 0).astype(jnp.int32))
    gathered = lax.all_gather(amplitudes, "bra", axis=0, tiled=True)

    def add_slot(slot_index, partial_value):
        tile_product = tile_term(gathered, integrals[slot_index])
        return add_block(partial_value, tile_product, local_rows[slot_index], tile_width)

    start_rows = jnp.zeros((gathered.shape[0], row_blocks * tile_width), jnp.float32)
    summed = lax.psum_scatter(
        lax.fori_loop(0, live_count, add_slot, start_rows), "ket", scatter_dimension=0, tiled=True
    )
    return summed / denominators


def solution(mesh):
    placed = (
        P(("bra", "ket"), None, None),
        P(("bra", "ket"), None),
        P("bra", "ket"),
        P("ket", "bra"),
    )
    return jax.shard_map(
        per_device, mesh=mesh, in_specs=placed, out_specs=P("ket", "bra"), check_vma=False
    )
```

profile of v0, /device:TPU:25, one launch (start us, length us, event | category | flops | bytes accessed | tf_op | source)
XLA Modules:
  0.0 299.0 jit_solution(13359739532237609844)
XLA Ops:
  6.5 0.0 all-reduce.3.cloned.1.call-start
  6.5 38.7 %all_gather.3 = f32[256,512]{1,0:T(8,128)S(1)} all-gather(f32[16,512]{1,0:T(8,128)} %param.8), channel_id=1, replica_groups=mesh['bra'=16,'ket'=64] {'bra'}, dimensions={0}, use_global_device_ids=true | all-gather | bytes 557056 | tf_op jit(solution)/shard_map/all_gather | solution.py:28
  45.2 1.3 subtract_bitcast_fusion
  46.5 1.6 broadcast_in_dim.3.clone
  48.1 13.5 %while.10 = (s32[]{:T(128)}, f32[256,2048]{1,0:T(8,128)}, s32[]{:T(128)}, s32[3]{0:T(128)S(1)}, f32[3,512,512]{2,1,0:T(8,128)}, /*index=5*/f32[256,512]{1,0:T(8,...) while((s32[]{:T(128)}, f32[256,2048]{1,0:T(8,128)}, s32[]{:T(128)}, ...), condition=%wide.region_2.0_spmd, body=%wide.region_1.0_spmd.sunk | while | flops 805437440 | bytes 6815957 | solution.py:36
  48.6 0.6 dynamic_slice.19
  49.9 1.1 constant_dynamic-slice_fusion.2
  51.0 0.2 copy.12
  51.2 2.2 fusion.11
  53.4 0.2 copy.13
  53.6 0.9 constant_dynamic-update-slice_fusion.2
  55.1 0.6 dynamic_slice.19
  56.4 1.1 constant_dynamic-slice_fusion.2
  57.5 0.2 copy.12
  57.7 2.2 fusion.11
  60.0 0.2 copy.13
  60.2 0.9 constant_dynamic-update-slice_fusion.2
  61.6 0.0 copy-start
  61.6 0.0 all-reduce.3.cloned.1.call-update
  61.6 1.3 dynamic-slice
  63.6 227.1 %all-reduce.3.cloned.1.call-done = f32[256,2048]{1,0:T(8,128)} async-done(((f32[256,2048]{1,0:T(8,128)}), f32[256,2048]{1,0:T(8,128)}) %all-reduce.3.cloned.1.call-update) | async-done | bytes 2097168
  290.6 0.0 copy-done
  290.7 1.5 dynamic-slice_divide_fusion
Async XLA Ops:
  6.5 284.1 %all-reduce.3.cloned.1.call-start = ((), (), s32[]{:S(2)}) async-start(), calls=%async_computation | async-start | bytes 4194304
  61.6 229.0 %copy-start = (f32[4,2048]{1,0:T(4,128)S(1)}, f32[4,2048]{1,0:T(4,128)}, u32[]{:S(2)}) copy-start(f32[4,2048]{1,0:T(4,128)} %param.9) | copy-start | bytes 98308
Sparse Core Ops, SparseCore 0:
  61.8 228.8 all-reduce.2
where the time goes:
time: 299 us
  waiting for transfers between devices  227 us (76%)
  blocking collectives  38.7 us (13%)
  between operations  14.1 us (5%)
  local copies, waits for them, and re-layouts  8.81 us (3%)
  matrix products  4.5 us (2%)
  loops' own time  3.06 us (1%)
    unnamed x2, waiting for transfers between devices  227 us
    all_gather x1, blocking collectives, per_device(): gathered = lax.all_gather(amplitudes, 'bra', axis=0, tiled=True)  38.7 us
  transfers between devices with their start and end apart: 1, of which 1 were waited for; matrix products, arithmetic and copies ran while one was open for 0% of the time, Pallas kernels for 0%

commit v1 on v0

v1 whole, which is shorter than its diff:
```python
import jax
import jax.numpy as jnp
from jax import lax
from jax.sharding import PartitionSpec as P

RS_MINOR = 256


def tile_term(amp_block, tile_now):
    return lax.dot_general(
        amp_block,
        tile_now,
        (((1,), (1,)), ((), ())),
        precision=lax.Precision.HIGHEST,
        preferred_element_type=jnp.float32,
    )


def partial_rows(gathered, integrals, local_rows, row_blocks):
    products = [tile_term(gathered, integrals[s]) for s in range(integrals.shape[0])]
    blocks = []
    for r in range(row_blocks):
        acc = jnp.zeros_like(products[0])
        for s, product in enumerate(products):
            acc = acc + jnp.where(local_rows[s] == r, product, 0.0)
        blocks.append(acc)
    return jnp.concatenate(blocks, axis=1)


def per_device(integrals, tile_place, amplitudes, denominators):
    tile_width = integrals.shape[1]
    row_blocks = denominators.shape[1] // tile_width
    local_rows = tile_place[:, 0] - lax.axis_index("bra") * row_blocks
    gathered = lax.all_gather(amplitudes, "bra", axis=0, tiled=True)
    partial = partial_rows(gathered, integrals, local_rows, row_blocks)
    occ, width = partial.shape
    summed = lax.psum_scatter(
        partial.reshape(occ * width // RS_MINOR, RS_MINOR), "ket", scatter_dimension=0, tiled=True
    )
    return summed.reshape(denominators.shape) / denominators


def solution(mesh):
    placed = (
        P(("bra", "ket"), None, None),
        P(("bra", "ket"), None),
        P("bra", "ket"),
        P("ket", "bra"),
    )
    return jax.shard_map(
        per_device, mesh=mesh, in_specs=placed, out_specs=P("ket", "bra"), check_vma=False
    )
```

time: 299 us -> 236 us (0.79)
  the two profiles are of different devices: /device:TPU:25 before, /device:TPU:16 now
where the time goes in v1:
time: 236 us
  waiting for transfers between devices  158 us (67%)
  blocking collectives  45.3 us (19%)
  between operations  21.1 us (9%)
  matrix products  7.09 us (3%)
  local copies, waits for them, and re-layouts  2.94 us (1%)
    reduce_scatter x1, waiting for transfers between devices, per_device(): lax.psum_scatter(partial.reshape(occ * width // RS_MINOR, RS_MINOR), 'ket...  158 us
    all_gather x1, blocking collectives, per_device(): gathered = lax.all_gather(amplitudes, 'bra', axis=0, tiled=True)  45.3 us
    dot_general x3, matrix products, tile_term(): lax.dot_general(amp_block, tile_now, (((1,), (1,)), ((), ())), precision=...  7.09 us
  transfers between devices with their start and end apart: 1, of which 1 were waited for; matrix products, arithmetic and copies ran while one was open for 0% of the time, Pallas kernels for 0%

profile of v1, /device:TPU:16, one launch (start us, length us, event | category | flops | bytes accessed | tf_op | source)
XLA Modules:
  0.0 236.1 jit_solution(12857225104774544267)
XLA Ops:
  6.5 0.0 reduce-scatter.2.cloned.1.call-start
  6.5 0.7 slice_subtract_fusion
  7.2 0.6 fusion.9
  15.5 45.3 %all_gather.3 = f32[256,512]{1,0:T(8,128)S(1)} all-gather(f32[16,512]{1,0:T(8,128)} %param.6), channel_id=1, replica_groups=mesh['bra'=16,'ket'=64] {'bra'}, dimensions={0}, use_global_device_ids=true | all-gather | bytes 557056 | tf_op jit(solution)/shard_map/all_gather | solution.py:34
  60.8 2.3 fusion.2
  63.0 2.3 fusion.4
  65.3 2.5 %select_add_fusion.3 = (f32[256,512]{1,0:T(8,128)S(1)}, f32[256,512]{1,0:T(8,128)S(1)}, f32[256,512]{1,0:T(8,128)S(1)}, f32[256,512]{1,0:T(8,128)S(1)}) fusion(f32[256,512]{1,0:T(8,128)S(1)} %fusion.2, f32[256,512]{1,0:T(8,128)S(1)} %fusion.4, pred[]{:T(512)} %bitcast.4, pred[]{:T(512)} %bitcast.2, pred[]{:T(512)} %bitcast, pred[]{:T(512)} %bitcast.14, ...), kind=kOutput, calls=%fused_computation.13 | convolution fusion | flops 807927808 | bytes 4724736 | tf_op jit(solution)/shard_map/dot_general | solution.py:10
  67.9 0.2 pad_maximum_fusion
  68.0 1.5 reshape.71
  69.5 0.0 copy-start
  69.5 0.0 reduce-scatter.2.cloned.1.call-update
  69.6 158.2 %reduce-scatter.2.cloned.1.call-done = f32[32,256]{1,0:T(8,128)} async-done(((f32[2048,256]{1,0:T(8,128)}), f32[32,256]{1,0:T(8,128)}) %reduce-scatter.2.cloned.1.call-update) | async-done | bytes 32784 | tf_op jit(solution)/shard_map/reduce_scatter | solution.py:37
  227.8 0.8 reshape.72
  228.6 0.0 copy-done
  228.6 0.6 div.3
Async XLA Ops:
  6.5 221.3 %reduce-scatter.2.cloned.1.call-start = ((), (), s32[]{:S(2)}) async-start(), calls=%async_computation.1 | async-start | bytes 2129920 | tf_op jit(solution)/shard_map/reduce_scatter | solution.py:37
  69.5 159.1 %copy-start = (f32[4,2048]{1,0:T(4,128)S(1)}, f32[4,2048]{1,0:T(4,128)}, u32[]{:S(2)}) copy-start(f32[4,2048]{1,0:T(4,128)} %param.7) | copy-start | bytes 98308
Sparse Core Ops, SparseCore 0:
  69.7 158.0 reduce-scatter.1

commit v2 on v1

--- a/solution.py
+++ b/solution.py
@@ -27,6 +27,41 @@
     return jnp.concatenate(blocks, axis=1)
 
 
+CHIP_X = 4
+CORES = 2
+
+
+def shifted(value, offset, size, stride, n):
+    pairs = []
+    for k in range(n):
+        coord = (k // stride) % size
+        dest = k + (((coord + offset) % size) - coord) * stride
+        pairs.append((k, dest))
+    return lax.ppermute(value, "ket", perm=pairs)
+
+
+def reduce_ket(partial):
+    n = lax.axis_size("ket")
+    n_y = n // (CHIP_X * CORES)
+    k = lax.axis_index("ket")
+    c = k % CORES
+    x = (k // CORES) % CHIP_X
+    y = k // (CORES * CHIP_X)
+    parts = partial.reshape(n_y, CHIP_X, CORES, -1, RS_MINOR)
+    keep = lax.dynamic_index_in_dim(parts, c, axis=2, keepdims=False)
+    send = lax.dynamic_index_in_dim(parts, 1 - c, axis=2, keepdims=False)
+    stage = keep + shifted(send, 1, CORES, 1, n)
+    total = lax.dynamic_index_in_dim(stage, x, axis=1, keepdims=False)
+    for s in range(1, CHIP_X):
+        piece = lax.dynamic_index_in_dim(stage, (x + s) % CHIP_X, axis=1, keepdims=False)
+        total = total + shifted(piece, s, CHIP_X, CORES, n)
+    stage = total
+    total = lax.dynamic_index_in_dim(stage, y, axis=0, keepdims=False)
+    for s in range(1, n_y):
+        piece = lax.dynamic_index_in_dim(stage, (y + s) % n_y, axis=0, keepdims=False)
+        total = total + shifted(piece, s, n_y, CORES * CHIP_X, n)
+    return total
+
 def per_device(integrals, tile_place, amplitudes, denominators):
     tile_width = integrals.shape[1]
     row_blocks = denominators.shape[1] // tile_width
@@ -34,9 +69,7 @@
     gathered = lax.all_gather(amplitudes, "bra", axis=0, tiled=True)
     partial = partial_rows(gathered, integrals, local_rows, row_blocks)
     occ, width = partial.shape
-    summed = lax.psum_scatter(
-        partial.reshape(occ * width // RS_MINOR, RS_MINOR), "ket", scatter_dimension=0, tiled=True
-    )
+    summed = reduce_ket(partial)
     return summed.reshape(denominators.shape) / denominators
 
 

time: 236 us -> 125 us (0.53)
  the two profiles are of different devices: /device:TPU:16 before, /device:TPU:8 now
where the time goes in v2:
time: 125 us; the launch traced here: 124 us
  blocking collectives  45.3 us (36%)
  starting transfers between devices  40.4 us (32%)
  waiting for transfers between devices  17.3 us (14%)
  between operations  8.09 us (6%)
  matrix products  7.1 us (6%)
  other arithmetic  3.59 us (3%)
  local copies, waits for them, and re-layouts  2.61 us (2%)
    all_gather x1, blocking collectives, per_device(): gathered = lax.all_gather(amplitudes, 'bra', axis=0, tiled=True)  45.3 us
    ppermute x11, starting transfers between devices, shifted(): return lax.ppermute(value, 'ket', perm=pairs)  40.4 us
    ppermute x11, waiting for transfers between devices, shifted(): return lax.ppermute(value, 'ket', perm=pairs)  17.3 us
    dot_general x3, matrix products, tile_term(): lax.dot_general(amp_block, tile_now, (((1,), (1,)), ((), ())), precision=...  7.1 us
  transfers between devices with their start and end apart: 11, of which 6 were waited for; matrix products, arithmetic and copies ran while one was open for 0% of the time, Pallas kernels for 0%

profile of v2, /device:TPU:8, one launch (start us, length us, event | category | flops | bytes accessed | tf_op | source)
XLA Modules:
  0.0 124.3 jit_solution(10693672038762697702)
XLA Ops:
  0.0 45.3 %all_gather.3 = f32[256,512]{1,0:T(8,128)S(1)} all-gather(f32[16,512]{1,0:T(8,128)} %param.6), channel_id=1, replica_groups=mesh['bra'=16,'ket'=64] {'bra'}, dimensions={0}, use_global_device_ids=true | all-gather | bytes 557056 | tf_op jit(solution)/shard_map/all_gather | solution.py:69
  45.3 2.3 %fusion.2 = f32[256,512]{1,0:T(8,128)S(1)} fusion(f32[256,512]{1,0:T(8,128)S(1)} %all_gather.3, f32[3,512,512]{2,1,0:T(8,128)} %param.4), kind=kOutput, calls=%fused_computation.4 | convolution fusion | flops 805306368 | bytes 2097152 | tf_op jit(solution)/shard_map/dot_general | solution.py:10
  47.6 2.3 %fusion.4 = f32[256,512]{1,0:T(8,128)S(1)} fusion(f32[256,512]{1,0:T(8,128)S(1)} %all_gather.3, f32[3,512,512]{2,1,0:T(8,128)} %param.4), kind=kOutput, calls=%fused_computation.6 | convolution fusion | flops 805306368 | bytes 2097152 | tf_op jit(solution)/shard_map/dot_general | solution.py:10
  49.9 0.6 fusion.17
  58.1 2.5 %select_add_fusion.3 = (f32[256,512]{1,0:T(8,128)S(1)}, f32[256,512]{1,0:T(8,128)S(1)}, f32[256,512]{1,0:T(8,128)S(1)}, f32[256,512]{1,0:T(8,128)S(1)}) fusion(f32[256,512]{1,0:T(8,128)S(1)} %fusion.2, f32[256,512]{1,0:T(8,128)S(1)} %fusion.4, pred[]{:T(512)} %bitcast.4, pred[]{:T(512)} %bitcast.2, pred[]{:T(512)} %bitcast, pred[]{:T(512)} %bitcast.14, ...), kind=kOutput, calls=%fused_computation.15 | convolution fusion | flops 807927808 | bytes 4724736 | tf_op jit(solution)/shard_map/dot_general | solution.py:10
  60.6 1.5 %pad_maximum_fusion = f32[256,2048]{1,0:T(8,128)} fusion(f32[256,512]{1,0:T(8,128)S(1)} %get-tuple-element.6, f32[256,512]{1,0:T(8,128)S(1)} %get-tuple-element.7, f32[256,512]{1,0:T(8,128)S(1)} %get-tuple-element.8, f32[256,512]{1,0:T(8,128)S(1)} %get-tuple-element.5), kind=kLoop, calls=%fused_computation | loop fusion | flops 1572864 | bytes 4194304 | tf_op jit(solution)/shard_map/concatenate | solution.py:27
  62.1 1.7 %reshape.71 = f32[8,4,2,32,256]{4,3,2,1,0:T(8,128)S(1)} reshape(f32[256,2048]{1,0:T(8,128)} %pad_maximum_fusion) | data formatting | bytes 4194304 | tf_op jit(solution)/shard_map/reshape | solution.py:50
  63.9 0.1 dynamic-slice_bitcast_fusion
  64.0 1.9 %collective-permute-start = (f32[8,4,32,256]{3,2,1,0:T(8,128)S(1)}, f32[8,4,32,256]{3,2,1,0:T(8,128)}, u32[]{:S(2)}, u32[]{:S(2)}) collective-permute-start(f32[8,4,32,256]{3,2,1,0:T(8,128)S(1)} %dynamic-slice_bitcast_fusion), channel_id=1, source_target_pairs={{0,1},{1,0},{2,3},{3,2},{4,5},{5,4},{6,7},{7,6},{8,9},{9,8},{10,11... | collective-permute-start | bytes 3145736 | tf_op jit(solution)/shard_map/ppermute | solution.py:40
  66.0 2.7 %collective-permute-done = f32[8,4,32,256]{3,2,1,0:T(8,128)} collective-permute-done((f32[8,4,32,256]{3,2,1,0:T(8,128)S(1)}, f32[8,4,32,256]{3,2,1,0:T(8,128)}, u32[]{:S(2)}, u32[]{:S(2)}) %collective-permute-start) | collective-permute-done | bytes 1048608 | tf_op jit(solution)/shard_map/ppermute | solution.py:40
  68.7 1.4 %bitcast_add_fusion = f32[8,4,32,256]{3,2,1,0:T(8,128)S(1)} fusion(f32[8,4,32,256]{3,2,1,0:T(8,128)} %collective-permute-done, f32[8,4,2,32,256]{4,3,2,1,0:T(8,128)S(1)} %reshape.71, s32[]{:T(128)S(6)} %select_n.202), kind=kLoop, calls=%fused_computation.1 | loop fusion | flops 262144 | bytes 3145732 | tf_op jit(solution)/shard_map/add | solution.py:53
  70.0 0.0 copy-start
  70.1 0.1 dynamic-slice_bitcast_fusion.3
  70.1 4.7 %collective-permute-start.3 = (f32[8,32,256]{2,1,0:T(8,128)S(1)}, f32[8,32,256]{2,1,0:T(8,128)S(1)}, u32[]{:S(2)}, u32[]{:S(2)}) collective-permute-start(f32[8,32,256]{2,1,0:T(8,128)S(1)} %get-tuple-element.10), channel_id=1, source_target_pairs={{0,6},{1,7},{2,0},{3,1},{4,2},{5,3},{6,4},{7,5},{8,14},{9,15},{10,... | collective-permute-start | bytes 786440 | tf_op jit(solution)/shard_map/ppermute | solution.py:40
  74.8 2.7 %collective-permute-start.2 = (f32[8,32,256]{2,1,0:T(8,128)S(1)}, f32[8,32,256]{2,1,0:T(8,128)S(1)}, u32[]{:S(2)}, u32[]{:S(2)}) collective-permute-start(f32[8,32,256]{2,1,0:T(8,128)S(1)} %get-tuple-element.11), channel_id=1, source_target_pairs={{0,4},{1,5},{2,6},{3,7},{4,0},{5,1},{6,2},{7,3},{8,12},{9,13},{10,... | collective-permute-start | bytes 786440 | tf_op jit(solution)/shard_map/ppermute | solution.py:40
  77.5 2.8 %collective-permute-start.1 = (f32[8,32,256]{2,1,0:T(8,128)S(1)}, f32[8,32,256]{2,1,0:T(8,128)S(1)}, u32[]{:S(2)}, u32[]{:S(2)}) collective-permute-start(f32[8,32,256]{2,1,0:T(8,128)S(1)} %get-tuple-element.9), channel_id=1, source_target_pairs={{0,2},{1,3},{2,4},{3,5},{4,6},{5,7},{6,0},{7,1},{8,10},{9,11},{10,... | collective-permute-start | bytes 786440 | tf_op jit(solution)/shard_map/ppermute | solution.py:40
  80.5 5.8 %collective-permute-done.3 = f32[8,32,256]{2,1,0:T(8,128)S(1)} collective-permute-done((f32[8,32,256]{2,1,0:T(8,128)S(1)}, f32[8,32,256]{2,1,0:T(8,128)S(1)}, u32[]{:S(2)}, u32[]{:S(2)}) %collective-permute-start.3) | collective-permute-done | bytes 262176 | tf_op jit(solution)/shard_map/ppermute | solution.py:40
  86.3 1.1 collective-permute-done.2
  87.4 4.4 %collective-permute-done.1 = f32[8,32,256]{2,1,0:T(8,128)S(1)} collective-permute-done((f32[8,32,256]{2,1,0:T(8,128)S(1)}, f32[8,32,256]{2,1,0:T(8,128)S(1)}, u32[]{:S(2)}, u32[]{:S(2)}) %collective-permute-start.1) | collective-permute-done | bytes 262176 | tf_op jit(solution)/shard_map/ppermute | solution.py:40
  91.9 0.1 fusion.10
  92.0 2.4 %collective-permute-start.10 = (f32[32,256]{1,0:T(8,128)S(1)}, f32[32,256]{1,0:T(8,128)S(1)}, u32[]{:S(2)}, u32[]{:S(2)}) collective-permute-start(f32[32,256]{1,0:T(8,128)S(1)} %get-tuple-element.13), channel_id=1, source_target_pairs={{0,56},{1,57},{2,58},{3,59},{4,60},{5,61},{6,62},{7,63},{8,0},{9,1... | collective-permute-start | bytes 98312 | tf_op jit(solution)/shard_map/ppermute | solution.py:40
  94.4 6.2 %collective-permute-start.9 = (f32[32,256]{1,0:T(8,128)S(1)}, f32[32,256]{1,0:T(8,128)S(1)}, u32[]{:S(2)}, u32[]{:S(2)}) collective-permute-start(f32[32,256]{1,0:T(8,128)S(1)} %get-tuple-element.14), channel_id=1, source_target_pairs={{0,48},{1,49},{2,50},{3,51},{4,52},{5,53},{6,54},{7,55},{8,56},{9,... | collective-permute-start | bytes 98312 | tf_op jit(solution)/shard_map/ppermute | solution.py:40
  100.5 3.9 %collective-permute-start.8 = (f32[32,256]{1,0:T(8,128)S(1)}, f32[32,256]{1,0:T(8,128)S(1)}, u32[]{:S(2)}, u32[]{:S(2)}) collective-permute-start(f32[32,256]{1,0:T(8,128)S(1)} %get-tuple-element.15), channel_id=1, source_target_pairs={{0,40},{1,41},{2,42},{3,43},{4,44},{5,45},{6,46},{7,47},{8,48},{9,... | collective-permute-start | bytes 98312 | tf_op jit(solution)/shard_map/ppermute | solution.py:40
  104.5 5.0 %collective-permute-start.7 = (f32[32,256]{1,0:T(8,128)S(1)}, f32[32,256]{1,0:T(8,128)S(1)}, u32[]{:S(2)}, u32[]{:S(2)}) collective-permute-start(f32[32,256]{1,0:T(8,128)S(1)} %get-tuple-element.16), channel_id=1, source_target_pairs={{0,32},{1,33},{2,34},{3,35},{4,36},{5,37},{6,38},{7,39},{8,40},{9,... | collective-permute-start | bytes 98312 | tf_op jit(solution)/shard_map/ppermute | solution.py:40
  109.5 3.7 %collective-permute-start.6 = (f32[32,256]{1,0:T(8,128)S(1)}, f32[32,256]{1,0:T(8,128)S(1)}, u32[]{:S(2)}, u32[]{:S(2)}) collective-permute-start(f32[32,256]{1,0:T(8,128)S(1)} %get-tuple-element.17), channel_id=1, source_target_pairs={{0,24},{1,25},{2,26},{3,27},{4,28},{5,29},{6,30},{7,31},{8,32},{9,... | collective-permute-start | bytes 98312 | tf_op jit(solution)/shard_map/ppermute | solution.py:40
  113.2 4.5 %collective-permute-start.5 = (f32[32,256]{1,0:T(8,128)S(1)}, f32[32,256]{1,0:T(8,128)S(1)}, u32[]{:S(2)}, u32[]{:S(2)}) collective-permute-start(f32[32,256]{1,0:T(8,128)S(1)} %get-tuple-element.18), channel_id=1, source_target_pairs={{0,16},{1,17},{2,18},{3,19},{4,20},{5,21},{6,22},{7,23},{8,24},{9,... | collective-permute-start | bytes 98312 | tf_op jit(solution)/shard_map/ppermute | solution.py:40
  117.7 0.0 collective-permute-done.9
  117.8 2.6 %collective-permute-start.4 = (f32[32,256]{1,0:T(8,128)S(1)}, f32[32,256]{1,0:T(8,128)S(1)}, u32[]{:S(2)}, u32[]{:S(2)}) collective-permute-start(f32[32,256]{1,0:T(8,128)S(1)} %get-tuple-element.12), channel_id=1, source_target_pairs={{0,8},{1,9},{2,10},{3,11},{4,12},{5,13},{6,14},{7,15},{8,16},{9,17... | collective-permute-start | bytes 98312 | tf_op jit(solution)/shard_map/ppermute | solution.py:40
  120.4 0.0 collective-permute-done.8
  120.4 0.9 collective-permute-done.5
  121.3 2.3 %collective-permute-done.4 = f32[32,256]{1,0:T(8,128)S(1)} collective-permute-done((f32[32,256]{1,0:T(8,128)S(1)}, f32[32,256]{1,0:T(8,128)S(1)}, u32[]{:S(2)}, u32[]{:S(2)}) %collective-permute-start.4) | collective-permute-done | bytes 32800 | tf_op jit(solution)/shard_map/ppermute | solution.py:40
  123.6 0.6 div.24
  (10 shorter events, 0.1 us)
Async XLA Ops:
  45.3 4.6 %copy-start.1 = (s32[3,2]{0,1:T(2,128)S(1)}, s32[3,2]{0,1:T(2,128)}, u32[]{:S(2)}) copy-start(s32[3,2]{0,1:T(2,128)} %param.5) | copy-start | bytes 76
  64.0 4.7 %collective-permute-start = (f32[8,4,32,256]{3,2,1,0:T(8,128)S(1)}, f32[8,4,32,256]{3,2,1,0:T(8,128)}, u32[]{:S(2)}, u32[]{:S(2)}) collective-permute-start(f32[8,4,32,256]{3,2,1,0:T(8,128)S(1)} %dynamic-slice_bitcast_fusion), channel_id=1, source_target_pairs={{0,1},{1,0},{2,3},{3,2},{4,5},{5,4},{6,7},{7,6},{8,9},{9,8},{10,11... | collective-permute-start | bytes 3145736 | tf_op jit(solution)/shard_map/ppermute | solution.py:40
  70.0 53.6 %copy-start = (f32[4,2048]{1,0:T(4,128)S(1)}, f32[4,2048]{1,0:T(4,128)}, u32[]{:S(2)}) copy-start(f32[4,2048]{1,0:T(4,128)} %param.7) | copy-start | bytes 98308
  70.1 16.2 %collective-permute-start.3 = (f32[8,32,256]{2,1,0:T(8,128)S(1)}, f32[8,32,256]{2,1,0:T(8,128)S(1)}, u32[]{:S(2)}, u32[]{:S(2)}) collective-permute-start(f32[8,32,256]{2,1,0:T(8,128)S(1)} %get-tuple-element.10), channel_id=1, source_target_pairs={{0,6},{1,7},{2,0},{3,1},{4,2},{5,3},{6,4},{7,5},{8,14},{9,15},{10,... | collective-permute-start | bytes 786440 | tf_op jit(solution)/shard_map/ppermute | solution.py:40
  74.8 12.6 %collective-permute-start.2 = (f32[8,32,256]{2,1,0:T(8,128)S(1)}, f32[8,32,256]{2,1,0:T(8,128)S(1)}, u32[]{:S(2)}, u32[]{:S(2)}) collective-permute-start(f32[8,32,256]{2,1,0:T(8,128)S(1)} %get-tuple-element.11), channel_id=1, source_target_pairs={{0,4},{1,5},{2,6},{3,7},{4,0},{5,1},{6,2},{7,3},{8,12},{9,13},{10,... | collective-permute-start | bytes 786440 | tf_op jit(solution)/shard_map/ppermute | solution.py:40
  77.5 14.4 %collective-permute-start.1 = (f32[8,32,256]{2,1,0:T(8,128)S(1)}, f32[8,32,256]{2,1,0:T(8,128)S(1)}, u32[]{:S(2)}, u32[]{:S(2)}) collective-permute-start(f32[8,32,256]{2,1,0:T(8,128)S(1)} %get-tuple-element.9), channel_id=1, source_target_pairs={{0,2},{1,3},{2,4},{3,5},{4,6},{5,7},{6,0},{7,1},{8,10},{9,11},{10,... | collective-permute-start | bytes 786440 | tf_op jit(solution)/shard_map/ppermute | solution.py:40
  92.0 21.2 %collective-permute-start.10 = (f32[32,256]{1,0:T(8,128)S(1)}, f32[32,256]{1,0:T(8,128)S(1)}, u32[]{:S(2)}, u32[]{:S(2)}) collective-permute-start(f32[32,256]{1,0:T(8,128)S(1)} %get-tuple-element.13), channel_id=1, source_target_pairs={{0,56},{1,57},{2,58},{3,59},{4,60},{5,61},{6,62},{7,63},{8,0},{9,1... | collective-permute-start | bytes 98312 | tf_op jit(solution)/shard_map/ppermute | solution.py:40
  94.4 23.4 %collective-permute-start.9 = (f32[32,256]{1,0:T(8,128)S(1)}, f32[32,256]{1,0:T(8,128)S(1)}, u32[]{:S(2)}, u32[]{:S(2)}) collective-permute-start(f32[32,256]{1,0:T(8,128)S(1)} %get-tuple-element.14), channel_id=1, source_target_pairs={{0,48},{1,49},{2,50},{3,51},{4,52},{5,53},{6,54},{7,55},{8,56},{9,... | collective-permute-start | bytes 98312 | tf_op jit(solution)/shard_map/ppermute | solution.py:40
  100.5 19.8 %collective-permute-start.8 = (f32[32,256]{1,0:T(8,128)S(1)}, f32[32,256]{1,0:T(8,128)S(1)}, u32[]{:S(2)}, u32[]{:S(2)}) collective-permute-start(f32[32,256]{1,0:T(8,128)S(1)} %get-tuple-element.15), channel_id=1, source_target_pairs={{0,40},{1,41},{2,42},{3,43},{4,44},{5,45},{6,46},{7,47},{8,48},{9,... | collective-permute-start | bytes 98312 | tf_op jit(solution)/shard_map/ppermute | solution.py:40
  104.5 15.9 %collective-permute-start.7 = (f32[32,256]{1,0:T(8,128)S(1)}, f32[32,256]{1,0:T(8,128)S(1)}, u32[]{:S(2)}, u32[]{:S(2)}) collective-permute-start(f32[32,256]{1,0:T(8,128)S(1)} %get-tuple-element.16), channel_id=1, source_target_pairs={{0,32},{1,33},{2,34},{3,35},{4,36},{5,37},{6,38},{7,39},{8,40},{9,... | collective-permute-start | bytes 98312 | tf_op jit(solution)/shard_map/ppermute | solution.py:40
  109.5 10.9 %collective-permute-start.6 = (f32[32,256]{1,0:T(8,128)S(1)}, f32[32,256]{1,0:T(8,128)S(1)}, u32[]{:S(2)}, u32[]{:S(2)}) collective-permute-start(f32[32,256]{1,0:T(8,128)S(1)} %get-tuple-element.17), channel_id=1, source_target_pairs={{0,24},{1,25},{2,26},{3,27},{4,28},{5,29},{6,30},{7,31},{8,32},{9,... | collective-permute-start | bytes 98312 | tf_op jit(solution)/shard_map/ppermute | solution.py:40
  113.2 8.0 %collective-permute-start.5 = (f32[32,256]{1,0:T(8,128)S(1)}, f32[32,256]{1,0:T(8,128)S(1)}, u32[]{:S(2)}, u32[]{:S(2)}) collective-permute-start(f32[32,256]{1,0:T(8,128)S(1)} %get-tuple-element.18), channel_id=1, source_target_pairs={{0,16},{1,17},{2,18},{3,19},{4,20},{5,21},{6,22},{7,23},{8,24},{9,... | collective-permute-start | bytes 98312 | tf_op jit(solution)/shard_map/ppermute | solution.py:40
  117.8 5.8 %collective-permute-start.4 = (f32[32,256]{1,0:T(8,128)S(1)}, f32[32,256]{1,0:T(8,128)S(1)}, u32[]{:S(2)}, u32[]{:S(2)}) collective-permute-start(f32[32,256]{1,0:T(8,128)S(1)} %get-tuple-element.12), channel_id=1, source_target_pairs={{0,8},{1,9},{2,10},{3,11},{4,12},{5,13},{6,14},{7,15},{8,16},{9,17... | collective-permute-start | bytes 98312 | tf_op jit(solution)/shard_map/ppermute | solution.py:40

commit v3 on v1

v3 whole, which is shorter than its diff:
```python
import jax
import jax.numpy as jnp
from jax import lax
from jax.sharding import Mesh, PartitionSpec as P

RS_MINOR = 256
CHIP_X = 4
CORES = 2
KET = ("y", "x", "core")


def tile_term(amp_block, tile_now):
    return lax.dot_general(
        amp_block,
        tile_now,
        (((1,), (1,)), ((), ())),
        precision=lax.Precision.HIGHEST,
        preferred_element_type=jnp.float32,
    )


def partial_rows(gathered, integrals, local_rows, row_blocks):
    products = [tile_term(gathered, integrals[s]) for s in range(integrals.shape[0])]
    blocks = []
    for r in range(row_blocks):
        acc = jnp.zeros_like(products[0])
        for s, product in enumerate(products):
            acc = acc + jnp.where(local_rows[s] == r, product, 0.0)
        blocks.append(acc)
    return jnp.concatenate(blocks, axis=1)


def gather_bra(amplitudes):
    return lax.all_gather(amplitudes, "bra", axis=0, tiled=True)


def reduce_ket(partial):
    n_y, n_x, n_c = (lax.axis_size(a) for a in KET)
    c = lax.axis_index("core")
    parts = partial.reshape(n_y, n_x, n_c, -1)
    keep = lax.dynamic_index_in_dim(parts, c, axis=2, keepdims=False)
    send = lax.dynamic_index_in_dim(parts, 1 - c, axis=2, keepdims=False)
    stage = keep + lax.ppermute(send, "core", perm=[(0, 1), (1, 0)])
    got = lax.all_to_all(stage, "x", 1, 1, tiled=True)
    stage = jnp.sum(got, axis=1)
    got = lax.all_to_all(stage, "y", 0, 0, tiled=True)
    return jnp.sum(got, axis=0)


def per_device(integrals, tile_place, amplitudes, denominators):
    tile_width = integrals.shape[1]
    row_blocks = denominators.shape[1] // tile_width
    local_rows = tile_place[:, 0] - lax.axis_index("bra") * row_blocks
    gathered = gather_bra(amplitudes)
    partial = partial_rows(gathered, integrals, local_rows, row_blocks)
    summed = reduce_ket(partial)
    return summed.reshape(denominators.shape) / denominators


def solution(mesh):
    n_bra, n_ket = mesh.devices.shape
    fine = Mesh(mesh.devices.reshape(n_bra, n_ket // (CHIP_X * CORES), CHIP_X, CORES), ("bra",) + KET)
    placed = (
        P(("bra",) + KET, None, None),
        P(("bra",) + KET, None),
        P("bra", KET),
        P(KET, "bra"),
    )
    return jax.shard_map(
        per_device, mesh=fine, in_specs=placed, out_specs=P(KET, "bra"), check_vma=False
    )
```

time: 236 us -> 112 us (0.47)
  the two profiles are of different devices: /device:TPU:16 before, /device:TPU:2 now
where the time goes in v3:
time: 112 us; the launch traced here: 111 us
  blocking collectives  81.5 us (73%)
  between operations  7.7 us (7%)
  matrix products  7.09 us (6%)
  local copies, waits for them, and re-layouts  6.63 us (6%)
  other arithmetic  3.78 us (3%)
  waiting for transfers between devices  2.63 us (2%)
  starting transfers between devices  1.92 us (2%)
    all_gather x1, blocking collectives, gather_bra(): return lax.all_gather(amplitudes, 'bra', axis=0, tiled=True)  45.3 us
    all_to_all x1, blocking collectives, reduce_ket(): got = lax.all_to_all(stage, 'x', 1, 1, tiled=True)  18.6 us
    all_to_all x1, blocking collectives, reduce_ket(): got = lax.all_to_all(stage, 'y', 0, 0, tiled=True)  17.6 us
    dot_general x3, matrix products, tile_term(): lax.dot_general(amp_block, tile_now, (((1,), (1,)), ((), ())), precision=...  7.09 us
    reshape x1, local copies, waits for them, and re-layouts, reduce_ket(): parts = partial.reshape(n_y, n_x, n_c, -1)  2.89 us
    ppermute x1, waiting for transfers between devices, reduce_ket(): stage = keep + lax.ppermute(send, 'core', perm=[(0, 1), (1, 0)])  2.63 us
    dynamic_slice x1, local copies, waits for them, and re-layouts, reduce_ket(): keep = lax.dynamic_index_in_dim(parts, c, axis=2, keepdims=False)  2.25 us
  transfers between devices with their start and end apart: 1, of which 1 were waited for; matrix products, arithmetic and copies ran while one was open for 0% of the time, Pallas kernels for 0%

profile of v3, /device:TPU:2, one launch (start us, length us, event | category | flops | bytes accessed | tf_op | source)
XLA Modules:
  0.0 111.2 jit_solution(17124231270463261161)
XLA Ops:
  0.0 0.7 slice_subtract_fusion
  0.7 0.7 fusion.9
  8.9 45.3 %all_gather.3 = f32[256,512]{1,0:T(8,128)S(1)} all-gather(f32[16,512]{1,0:T(8,128)} %param.6), channel_id=1, replica_groups=mesh['bra'=16,'y'=8,'x'=4,'core'=2] {'bra'}, dimensions={0}, use_global_device_ids=true | all-gather | bytes 557056 | tf_op jit(solution)/shard_map/all_gather | solution.py:34
  54.2 2.3 %fusion.2 = f32[256,512]{1,0:T(8,128)S(1)} fusion(f32[256,512]{1,0:T(8,128)S(1)} %all_gather.3, f32[3,512,512]{2,1,0:T(8,128)} %param.4), kind=kOutput, calls=%fused_computation.4 | convolution fusion | flops 805306368 | bytes 2097152 | tf_op jit(solution)/shard_map/dot_general | solution.py:13
  56.5 2.3 %fusion.4 = f32[256,512]{1,0:T(8,128)S(1)} fusion(f32[256,512]{1,0:T(8,128)S(1)} %all_gather.3, f32[3,512,512]{2,1,0:T(8,128)} %param.4), kind=kOutput, calls=%fused_computation.6 | convolution fusion | flops 805306368 | bytes 2097152 | tf_op jit(solution)/shard_map/dot_general | solution.py:13
  58.8 2.5 %select_add_fusion.3 = (f32[256,512]{1,0:T(8,128)S(1)}, f32[256,512]{1,0:T(8,128)S(1)}, f32[256,512]{1,0:T(8,128)S(1)}, f32[256,512]{1,0:T(8,128)S(1)}) fusion(f32[256,512]{1,0:T(8,128)S(1)} %fusion.2, f32[256,512]{1,0:T(8,128)S(1)} %fusion.4, pred[]{:T(512)} %bitcast.4, pred[]{:T(512)} %bitcast.2, pred[]{:T(512)} %bitcast, pred[]{:T(512)} %bitcast.14, ...), kind=kOutput, calls=%fused_computation.15 | convolution fusion | flops 807927808 | bytes 4724736 | tf_op jit(solution)/shard_map/dot_general | solution.py:13
  61.3 1.5 %pad_maximum_fusion = f32[256,2048]{1,0:T(8,128)} fusion(f32[256,512]{1,0:T(8,128)S(1)} %get-tuple-element.8, f32[256,512]{1,0:T(8,128)S(1)} %get-tuple-element.9, f32[256,512]{1,0:T(8,128)S(1)} %get-tuple-element.10, f32[256,512]{1,0:T(8,128)S(1)} %get-tuple-element.7), kind=kLoop, calls=%fused_computation | loop fusion | flops 1572864 | bytes 4194304 | tf_op jit(solution)/shard_map/concatenate | solution.py:30
  62.9 2.9 %reshape.73 = f32[8,4,2,8192]{3,2,1,0:T(2,128)S(1)} reshape(f32[256,2048]{1,0:T(8,128)} %pad_maximum_fusion) | data formatting | bytes 4194304 | tf_op jit(solution)/shard_map/reshape | solution.py:40
  65.8 2.3 %constant_dynamic-slice_fusion.1 = (f32[8,4,1,8192]{3,2,1,0:T(1,128)S(1)}, f32[8,4,1,8192]{3,2,1,0:T(1,128)S(1)}) fusion(f32[8,4,2,8192]{3,2,1,0:T(2,128)S(1)} %reshape.73, s32[]{:T(128)S(6)} %select_n.105, s32[]{:T(128)S(6)} %select_n.106), kind=kLoop, calls=%fused_computation.17 | loop fusion | bytes 4194312 | tf_op jit(solution)/shard_map/jit(dynamic_index_in_dim)/dynamic_slice | solution.py:41
  68.0 0.6 copy.9
  68.6 1.9 %collective-permute-start = (f32[8,4,8192]{2,0,1:T(8,128)S(1)}, f32[8,4,8192]{2,0,1:T(8,128)S(1)}, u32[]{:S(2)}, u32[]{:S(2)}) collective-permute-start(f32[8,4,8192]{2,0,1:T(8,128)S(1)} %bitcast.31), channel_id=1, source_target_pairs={{0,1},{1,0},{2,3},{3,2},{4,5},{5,4},{6,7},{7,6},{8,9},{9,8},{10,11... | collective-permute-start | bytes 3145736 | tf_op jit(solution)/shard_map/ppermute | solution.py:43
  70.6 2.6 %collective-permute-done = f32[8,4,8192]{2,0,1:T(8,128)S(1)} collective-permute-done((f32[8,4,8192]{2,0,1:T(8,128)S(1)}, f32[8,4,8192]{2,0,1:T(8,128)S(1)}, u32[]{:S(2)}, u32[]{:S(2)}) %collective-permute-start) | collective-permute-done | bytes 1048608 | tf_op jit(solution)/shard_map/ppermute | solution.py:43
  73.2 0.7 bitcast_add_fusion
  73.9 0.0 copy-start
  73.9 18.6 %all_to_all.14 = f32[8,4,8192]{2,0,1:T(8,128)S(1)} all-to-all(f32[8,4,8192]{2,0,1:T(8,128)S(1)} %bitcast_add_fusion), channel_id=1, replica_groups=mesh['bra'=16,'y'=8,'x'=4,'core'=2] {'x'}, dimensions={1} | all-to-all | bytes 2097152 | tf_op jit(solution)/shard_map/all_to_all | solution.py:44
  92.4 0.1 reduce_sum.18
  92.5 0.2 all_to_all.10
  92.7 17.6 %all_to_all.15 = f32[8,1,8192]{2,1,0:T(1,128)S(1)} all-to-all(f32[8,1,8192]{2,1,0:T(1,128)S(1)} %all_to_all.10), channel_id=1, replica_groups=mesh['bra'=16,'y'=8,'x'=4,'core'=2] {'y'}, dimensions={0} | all-to-all | bytes 524288 | tf_op jit(solution)/shard_map/all_to_all | solution.py:46
  110.3 0.2 reduce_sum.19
  110.6 0.0 copy-done
  110.6 0.6 div.3
  (1 shorter events, 0.0 us)
Async XLA Ops:
  68.6 4.6 %collective-permute-start = (f32[8,4,8192]{2,0,1:T(8,128)S(1)}, f32[8,4,8192]{2,0,1:T(8,128)S(1)}, u32[]{:S(2)}, u32[]{:S(2)}) collective-permute-start(f32[8,4,8192]{2,0,1:T(8,128)S(1)} %bitcast.31), channel_id=1, source_target_pairs={{0,1},{1,0},{2,3},{3,2},{4,5},{5,4},{6,7},{7,6},{8,9},{9,8},{10,11... | collective-permute-start | bytes 3145736 | tf_op jit(solution)/shard_map/ppermute | solution.py:43
  73.9 36.7 %copy-start = (f32[4,2048]{1,0:T(4,128)S(1)}, f32[4,2048]{1,0:T(4,128)}, u32[]{:S(2)}) copy-start(f32[4,2048]{1,0:T(4,128)} %param.7) | copy-start | bytes 98308

commit v4 on v3

--- a/solution.py
+++ b/solution.py
@@ -31,7 +31,9 @@
 
 
 def gather_bra(amplitudes):
-    return lax.all_gather(amplitudes, "bra", axis=0, tiled=True)
+    n_bra = lax.axis_size("bra")
+    copies = jnp.broadcast_to(amplitudes[None], (n_bra,) + amplitudes.shape)
+    return lax.all_to_all(copies, "bra", 0, 0, tiled=True).reshape(-1, amplitudes.shape[1])
 
 
 def reduce_ket(partial):

time: 112 us -> 107 us (0.955)
  blocking collectives: 81.5 us -> 36.2 us
  waiting for transfers between devices: 2.63 us -> 22.8 us
  starting transfers between devices: 1.92 us -> 20.8 us
  local copies, waits for them, and re-layouts: 6.63 us -> 8.2 us
    all_gather x1 -> x0, blocking collectives: 45.3 us -> none  [gather_bra(): return lax.all_gather(amplitudes, 'bra', axis=0, tiled=True)]
    all_to_all x0 -> x1, waiting for transfers between devices: none -> 20.1 us  [gather_bra(): lax.all_to_all(copies, 'bra', 0, 0, tiled=True)]
    all_to_all x0 -> x1, starting transfers between devices: none -> 18.9 us  [gather_bra(): lax.all_to_all(copies, 'bra', 0, 0, tiled=True)]
    broadcast_in_dim x0 -> x1, local copies, waits for them, and re-layouts: none -> 1.59 us  [gather_bra(): copies = jnp.broadcast_to(amplitudes[None], (n_bra,) + amplitudes.shape)]
  transfers between devices with their start and end apart: 1 -> 2, of which waited for: 1 -> 2; matrix products, arithmetic and copies ran while one was open for 0% -> 1% of each run, Pallas kernels for 0% -> 0%
where the time goes in v4:
time: 107 us
  blocking collectives  36.2 us (34%)
  waiting for transfers between devices  22.8 us (21%)
  starting transfers between devices  20.8 us (19%)
  local copies, waits for them, and re-layouts  8.2 us (8%)
  between operations  7.73 us (7%)
  matrix products  7.09 us (7%)
  other arithmetic  3.78 us (4%)
    all_to_all x1, waiting for transfers between devices, gather_bra(): lax.all_to_all(copies, 'bra', 0, 0, tiled=True)  20.1 us
    all_to_all x1, starting transfers between devices, gather_bra(): lax.all_to_all(copies, 'bra', 0, 0, tiled=True)  18.9 us
    all_to_all x1, blocking collectives, reduce_ket(): got = lax.all_to_all(stage, 'x', 1, 1, tiled=True)  18.6 us
    all_to_all x1, blocking collectives, reduce_ket(): got = lax.all_to_all(stage, 'y', 0, 0, tiled=True)  17.6 us
    dot_general x3, matrix products, tile_term(): lax.dot_general(amp_block, tile_now, (((1,), (1,)), ((), ())), precision=...  7.09 us
    reshape x1, local copies, waits for them, and re-layouts, reduce_ket(): parts = partial.reshape(n_y, n_x, n_c, -1)  2.89 us
    ppermute x1, waiting for transfers between devices, reduce_ket(): stage = keep + lax.ppermute(send, 'core', perm=[(0, 1), (1, 0)])  2.63 us
    dynamic_slice x1, local copies, waits for them, and re-layouts, reduce_ket(): keep = lax.dynamic_index_in_dim(parts, c, axis=2, keepdims=False)  2.25 us
  transfers between devices with their start and end apart: 2, of which 2 were waited for; matrix products, arithmetic and copies ran while one was open for 1% of the time, Pallas kernels for 0%

profile of v4, /device:TPU:2, one launch (start us, length us, event | category | flops | bytes accessed | tf_op | source)
XLA Modules:
  0.0 106.5 jit_solution(8317057700385593274)
XLA Ops:
  0.0 1.6 %broadcast_in_dim.21 = f32[16,16,512]{2,1,0:T(8,128)} broadcast(f32[16,512]{1,0:T(8,128)} %param.6), dimensions={1,2} | broadcast | bytes 557056 | tf_op jit(solution)/shard_map/broadcast_in_dim | solution.py:35
  1.6 18.9 %all-to-all-start = ((f32[16,16,512]{2,1,0:T(8,128)}), f32[16,16,512]{2,1,0:T(8,128)S(1)}, u32[]{:S(2)}, u32[]{:S(2)}) async-start(f32[16,16,512]{2,1,0:T(8,128)} %broadcast_in_dim.21), calls=%async_computation | async-start | bytes 1048576 | tf_op jit(solution)/shard_map/all_to_all | solution.py:36
  20.5 0.7 slice_subtract_fusion
  21.2 0.6 fusion.9
  29.4 20.1 %all-to-all-done = f32[16,16,512]{2,1,0:T(8,128)S(1)} async-done(((f32[16,16,512]{2,1,0:T(8,128)}), f32[16,16,512]{2,1,0:T(8,128)S(1)}, u32[]{:S(2)}, u32[]{:S(2)}) %all-to-all-start) | async-done | bytes 524320 | tf_op jit(solution)/shard_map/all_to_all | solution.py:36
  49.6 2.3 %fusion.2 = f32[256,512]{1,0:T(8,128)S(1)} fusion(f32[256,512]{1,0:T(8,128)S(1)} %bitcast.32, f32[3,512,512]{2,1,0:T(8,128)} %param.4), kind=kOutput, calls=%fused_computation.4 | convolution fusion | flops 805306368 | bytes 2097152 | tf_op jit(solution)/shard_map/dot_general | solution.py:13
  51.8 2.3 %fusion.4 = f32[256,512]{1,0:T(8,128)S(1)} fusion(f32[256,512]{1,0:T(8,128)S(1)} %bitcast.33, f32[3,512,512]{2,1,0:T(8,128)} %param.4), kind=kOutput, calls=%fused_computation.6 | convolution fusion | flops 805306368 | bytes 2097152 | tf_op jit(solution)/shard_map/dot_general | solution.py:13
  54.1 2.5 %select_add_fusion.3 = (f32[256,512]{1,0:T(8,128)S(1)}, f32[256,512]{1,0:T(8,128)S(1)}, f32[256,512]{1,0:T(8,128)S(1)}, f32[256,512]{1,0:T(8,128)S(1)}) fusion(f32[256,512]{1,0:T(8,128)S(1)} %fusion.2, f32[256,512]{1,0:T(8,128)S(1)} %fusion.4, pred[]{:T(512)} %bitcast.5, pred[]{:T(512)} %bitcast.3, pred[]{:T(512)} %bitcast, pred[]{:T(512)} %bitcast.15, ...), kind=kOutput, calls=%fused_computation.15 | convolution fusion | flops 807927808 | bytes 4724736 | tf_op jit(solution)/shard_map/dot_general | solution.py:13
  56.7 1.5 %pad_maximum_fusion = f32[256,2048]{1,0:T(8,128)} fusion(f32[256,512]{1,0:T(8,128)S(1)} %get-tuple-element.8, f32[256,512]{1,0:T(8,128)S(1)} %get-tuple-element.9, f32[256,512]{1,0:T(8,128)S(1)} %get-tuple-element.10, f32[256,512]{1,0:T(8,128)S(1)} %get-tuple-element.7), kind=kLoop, calls=%fused_computation | loop fusion | flops 1572864 | bytes 4194304 | tf_op jit(solution)/shard_map/concatenate | solution.py:30
  58.2 2.9 %reshape.78 = f32[8,4,2,8192]{3,2,1,0:T(2,128)S(1)} reshape(f32[256,2048]{1,0:T(8,128)} %pad_maximum_fusion) | data formatting | bytes 4194304 | tf_op jit(solution)/shard_map/reshape | solution.py:42
  61.1 2.3 %constant_dynamic-slice_fusion.1 = (f32[8,4,1,8192]{3,2,1,0:T(1,128)S(1)}, f32[8,4,1,8192]{3,2,1,0:T(1,128)S(1)}) fusion(f32[8,4,2,8192]{3,2,1,0:T(2,128)S(1)} %reshape.78, s32[]{:T(128)S(6)} %select_n.105, s32[]{:T(128)S(6)} %select_n.106), kind=kLoop, calls=%fused_computation.17 | loop fusion | bytes 4194312 | tf_op jit(solution)/shard_map/jit(dynamic_index_in_dim)/dynamic_slice | solution.py:43
  63.3 0.6 copy.9
  64.0 1.9 %collective-permute-start = (f32[8,4,8192]{2,0,1:T(8,128)S(1)}, f32[8,4,8192]{2,0,1:T(8,128)S(1)}, u32[]{:S(2)}, u32[]{:S(2)}) collective-permute-start(f32[8,4,8192]{2,0,1:T(8,128)S(1)} %bitcast.35), channel_id=1, source_target_pairs={{0,1},{1,0},{2,3},{3,2},{4,5},{5,4},{6,7},{7,6},{8,9},{9,8},{10,11... | collective-permute-start | bytes 3145736 | tf_op jit(solution)/shard_map/ppermute | solution.py:45
  65.9 2.6 %collective-permute-done = f32[8,4,8192]{2,0,1:T(8,128)S(1)} collective-permute-done((f32[8,4,8192]{2,0,1:T(8,128)S(1)}, f32[8,4,8192]{2,0,1:T(8,128)S(1)}, u32[]{:S(2)}, u32[]{:S(2)}) %collective-permute-start) | collective-permute-done | bytes 1048608 | tf_op jit(solution)/shard_map/ppermute | solution.py:45
  68.5 0.7 bitcast_add_fusion
  69.2 0.0 copy-start
  69.2 18.6 %all_to_all.19 = f32[8,4,8192]{2,0,1:T(8,128)S(1)} all-to-all(f32[8,4,8192]{2,0,1:T(8,128)S(1)} %bitcast_add_fusion), channel_id=1, replica_groups=mesh['bra'=16,'y'=8,'x'=4,'core'=2] {'x'}, dimensions={1} | all-to-all | bytes 2097152 | tf_op jit(solution)/shard_map/all_to_all | solution.py:46
  87.8 0.1 reduce_sum.18
  87.9 0.2 all_to_all.14
  88.0 17.6 %all_to_all.20 = f32[8,1,8192]{2,1,0:T(1,128)S(1)} all-to-all(f32[8,1,8192]{2,1,0:T(1,128)S(1)} %all_to_all.14), channel_id=1, replica_groups=mesh['bra'=16,'y'=8,'x'=4,'core'=2] {'y'}, dimensions={0} | all-to-all | bytes 524288 | tf_op jit(solution)/shard_map/all_to_all | solution.py:48
  105.7 0.2 reduce_sum.19
  105.9 0.0 copy-done
  105.9 0.6 div.3
  (1 shorter events, 0.0 us)
Async XLA Ops:
  1.6 48.0 %all-to-all-start = ((f32[16,16,512]{2,1,0:T(8,128)}), f32[16,16,512]{2,1,0:T(8,128)S(1)}, u32[]{:S(2)}, u32[]{:S(2)}) async-start(f32[16,16,512]{2,1,0:T(8,128)} %broadcast_in_dim.21), calls=%async_computation | async-start | bytes 1048576 | tf_op jit(solution)/shard_map/all_to_all | solution.py:36
  64.0 4.6 %collective-permute-start = (f32[8,4,8192]{2,0,1:T(8,128)S(1)}, f32[8,4,8192]{2,0,1:T(8,128)S(1)}, u32[]{:S(2)}, u32[]{:S(2)}) collective-permute-start(f32[8,4,8192]{2,0,1:T(8,128)S(1)} %bitcast.35), channel_id=1, source_target_pairs={{0,1},{1,0},{2,3},{3,2},{4,5},{5,4},{6,7},{7,6},{8,9},{9,8},{10,11... | collective-permute-start | bytes 3145736 | tf_op jit(solution)/shard_map/ppermute | solution.py:45
  69.2 36.7 %copy-start = (f32[4,2048]{1,0:T(4,128)S(1)}, f32[4,2048]{1,0:T(4,128)}, u32[]{:S(2)}) copy-start(f32[4,2048]{1,0:T(4,128)} %param.7) | copy-start | bytes 98308

commit v5 on v4

--- a/solution.py
+++ b/solution.py
@@ -14,7 +14,7 @@
         amp_block,
         tile_now,
         (((1,), (1,)), ((), ())),
-        precision=lax.Precision.HIGHEST,
+        precision=lax.Precision.HIGH,
         preferred_element_type=jnp.float32,
     )
 
@@ -36,13 +36,7 @@
     return lax.all_to_all(copies, "bra", 0, 0, tiled=True).reshape(-1, amplitudes.shape[1])
 
 
-def reduce_ket(partial):
-    n_y, n_x, n_c = (lax.axis_size(a) for a in KET)
-    c = lax.axis_index("core")
-    parts = partial.reshape(n_y, n_x, n_c, -1)
-    keep = lax.dynamic_index_in_dim(parts, c, axis=2, keepdims=False)
-    send = lax.dynamic_index_in_dim(parts, 1 - c, axis=2, keepdims=False)
-    stage = keep + lax.ppermute(send, "core", perm=[(0, 1), (1, 0)])
+def reduce_plane(stage):
     got = lax.all_to_all(stage, "x", 1, 1, tiled=True)
     stage = jnp.sum(got, axis=1)
     got = lax.all_to_all(stage, "y", 0, 0, tiled=True)
@@ -53,9 +47,15 @@
     tile_width = integrals.shape[1]
     row_blocks = denominators.shape[1] // tile_width
     local_rows = tile_place[:, 0] - lax.axis_index("bra") * row_blocks
-    gathered = gather_bra(amplitudes)
-    partial = partial_rows(gathered, integrals, local_rows, row_blocks)
-    summed = reduce_ket(partial)
+    n_y, n_x, n_c = (lax.axis_size(a) for a in KET)
+    c = lax.axis_index("core")
+    gathered = gather_bra(amplitudes).reshape(n_y, n_x, n_c, -1, tile_width)
+    own = lax.dynamic_index_in_dim(gathered, c, axis=2, keepdims=False).reshape(-1, tile_width)
+    other = lax.dynamic_index_in_dim(gathered, 1 - c, axis=2, keepdims=False).reshape(-1, tile_width)
+    sent = partial_rows(other, integrals, local_rows, row_blocks)
+    arrived = lax.ppermute(sent, "core", perm=[(0, 1), (1, 0)])
+    stage = partial_rows(own, integrals, local_rows, row_blocks) + arrived
+    summed = reduce_plane(stage.reshape(n_y, n_x, -1))
     return summed.reshape(denominators.shape) / denominators
 
 

time: 107 us -> 105 us (0.981)
  matrix products: 7.09 us -> 4.13 us
  waiting for transfers between devices: 22.8 us -> 20.2 us
  local copies, waits for them, and re-layouts: 8.2 us -> 9.81 us
  blocking collectives: 36.2 us -> 37.3 us
    dot_general x3 -> x6, matrix products: 7.09 us -> 4.13 us  [tile_term(): lax.dot_general(amp_block, tile_now, (((1,), (1,)), ((), ())), precision=...]
    ppermute x1, waiting for transfers between devices: 2.63 us -> 0.01 us  [per_device(): arrived = lax.ppermute(sent, 'core', perm=[(0, 1), (1, 0)])]
    another operation x0 -> x1, local copies, waits for them, and re-layouts: none -> 1.97 us  [per_device(): gathered = gather_bra(amplitudes).reshape(n_y, n_x, n_c, -1, tile_width)]
    all_to_all x2, blocking collectives: 36.2 us -> 37.3 us  [the longest x1 18.9 us: reduce_plane(): got = lax.all_to_all(stage, 'x', 1, 1, tiled=True)]
    dynamic_slice x2 -> x1, local copies, waits for them, and re-layouts: 2.86 us -> 1.89 us  [per_device(): lax.dynamic_index_in_dim(gathered, c, axis=2, keepdims=False)]
    reshape x1 -> x4, local copies, waits for them, and re-layouts: 2.89 us -> 3.34 us  [the longest x2 1.25 us: per_device(): summed = reduce_plane(stage.reshape(n_y, n_x, -1))]
  transfers between devices with their start and end apart: 2 -> 2, of which waited for: 2 -> 1; matrix products, arithmetic and copies ran while one was open for 1% -> 4% of each run, Pallas kernels for 0% -> 0%
where the time goes in v5:
time: 105 us; the launch traced here: 104 us
  blocking collectives  37.3 us (36%)
  starting transfers between devices  20.8 us (20%)
  waiting for transfers between devices  20.2 us (19%)
  local copies, waits for them, and re-layouts  9.81 us (9%)
  between operations  7.75 us (7%)
  matrix products  4.13 us (4%)
  other arithmetic  4 us (4%)
    all_to_all x1, waiting for transfers between devices, gather_bra(): lax.all_to_all(copies, 'bra', 0, 0, tiled=True)  20.2 us
    all_to_all x1, blocking collectives, reduce_plane(): got = lax.all_to_all(stage, 'x', 1, 1, tiled=True)  18.9 us
    all_to_all x1, starting transfers between devices, gather_bra(): lax.all_to_all(copies, 'bra', 0, 0, tiled=True)  18.9 us
    all_to_all x1, blocking collectives, reduce_plane(): got = lax.all_to_all(stage, 'y', 0, 0, tiled=True)  18.3 us
    dot_general x6, matrix products, tile_term(): lax.dot_general(amp_block, tile_now, (((1,), (1,)), ((), ())), precision=...  4.13 us
  transfers between devices with their start and end apart: 2, of which 1 were waited for; matrix products, arithmetic and copies ran while one was open for 4% of the time, Pallas kernels for 0%

profile of v5, /device:TPU:2, one launch (start us, length us, event | category | flops | bytes accessed | tf_op | source)
XLA Modules:
  0.0 104.0 jit_solution(6170884317646899793)
XLA Ops:
  0.0 0.0 copy-start
  0.0 1.7 %broadcast_in_dim.33 = f32[16,16,512]{2,1,0:T(8,128)} broadcast(f32[16,512]{1,0:T(8,128)} %param.6), dimensions={1,2} | broadcast | bytes 557056 | tf_op jit(solution)/shard_map/broadcast_in_dim | solution.py:35
  1.8 18.9 %all-to-all-start = ((f32[16,16,512]{2,1,0:T(8,128)}), f32[16,16,512]{2,1,0:T(8,128)}, u32[]{:S(2)}, u32[]{:S(2)}) async-start(f32[16,16,512]{2,1,0:T(8,128)} %broadcast_in_dim.33), calls=%async_computation | async-start | bytes 1048576 | tf_op jit(solution)/shard_map/all_to_all | solution.py:36
  20.7 0.7 slice_subtract_fusion
  21.4 0.7 fusion.18
  29.6 20.2 %all-to-all-done = f32[16,16,512]{2,1,0:T(8,128)} async-done(((f32[16,16,512]{2,1,0:T(8,128)}), f32[16,16,512]{2,1,0:T(8,128)}, u32[]{:S(2)}, u32[]{:S(2)}) %all-to-all-start) | async-done | bytes 524320 | tf_op jit(solution)/shard_map/all_to_all | solution.py:36
  49.8 2.0 %reshape_reshape.3 = f32[8,4,2,4,512]{4,3,2,1,0:T(4,128)} reshape(f32[16,16,512]{2,1,0:T(8,128)} %all-to-all-done) | data formatting | bytes 1048576 | tf_op jit(solution)/shard_map/reshape;reshape | solution.py:52
  51.8 1.9 %constant_dynamic-slice_fusion.1 = (f32[8,4,1,4,512]{4,3,2,1,0:T(4,128)}, f32[8,4,1,4,512]{4,3,2,1,0:T(4,128)}) fusion(f32[8,4,2,4,512]{4,3,2,1,0:T(4,128)} %reshape_reshape.3, s32[]{:T(128)S(6)} %select_n.130, s32[]{:T(128)S(6)} %select_n.154), kind=kLoop, calls=%fused_computation.29 | loop fusion | bytes 1048584 | tf_op jit(solution)/shard_map/jit(dynamic_index_in_dim)/dynamic_slice | solution.py:53
  53.7 1.0 %reshape.83 = f32[128,512]{1,0:T(8,128)S(1)} reshape(f32[8,4,1,4,512]{4,3,2,1,0:T(4,128)} %get-tuple-element.14) | data formatting | bytes 524288 | tf_op jit(solution)/shard_map/reshape | solution.py:54
  54.7 0.0 copy-done
  54.7 0.7 fusion.4
  55.4 0.7 fusion.8
  56.1 0.7 select_add_fusion.3
  56.8 1.0 %pad_maximum_fusion = f32[128,2048]{1,0:T(8,128)} fusion(f32[128,512]{1,0:T(8,128)S(1)} %get-tuple-element.10, f32[128,512]{1,0:T(8,128)S(1)} %get-tuple-element.11, f32[128,512]{1,0:T(8,128)S(1)} %get-tuple-element.12, f32[128,512]{1,0:T(8,128)S(1)} %get-tuple-element.9), kind=kLoop, calls=%fused_computation.1 | loop fusion | flops 786432 | bytes 2097152 | tf_op jit(solution)/shard_map/concatenate | solution.py:30
  57.9 1.9 %collective-permute-start = (f32[128,2048]{1,0:T(8,128)}, f32[128,2048]{1,0:T(8,128)}, u32[]{:S(2)}, u32[]{:S(2)}) collective-permute-start(f32[128,2048]{1,0:T(8,128)} %pad_maximum_fusion), channel_id=1, source_target_pairs={{0,1},{1,0},{2,3},{3,2},{4,5},{5,4},{6,7},{7,6},{8,9},{9,8},{10,11... | collective-permute-start | bytes 3145736 | tf_op jit(solution)/shard_map/ppermute | solution.py:56
  59.8 1.0 %reshape.82 = f32[128,512]{1,0:T(8,128)S(1)} reshape(f32[8,4,1,4,512]{4,3,2,1,0:T(4,128)} %get-tuple-element.13) | data formatting | bytes 524288 | tf_op jit(solution)/shard_map/reshape | solution.py:53
  60.8 0.7 fusion.6
  61.5 0.7 fusion.10
  62.2 0.7 select_add_fusion.7
  62.9 0.0 collective-permute-done
  62.9 1.4 %maximum_add_fusion = f32[128,2048]{1,0:T(8,128)S(1)} fusion(f32[128,2048]{1,0:T(8,128)} %collective-permute-done, f32[128,512]{1,0:T(8,128)S(1)} %get-tuple-element.6, f32[128,512]{1,0:T(8,128)S(1)} %get-tuple-element.7, f32[128,512]{1,0:T(8,128)S(1)} %get-tuple-element.8, f32[128,512]{1,0:T(8,128)S(1)} %get-tuple-element.5), kind=kLoop, calls=%fused_computation | loop fusion | flops 1048576 | bytes 3145728 | tf_op jit(solution)/shard_map/add | solution.py:57
  64.3 0.6 reshape.84
  65.0 0.0 copy-start.1
  65.0 0.6 copy.5
  65.6 18.9 %all_to_all.19 = f32[8,4,8192]{2,0,1:T(8,128)S(1)} all-to-all(f32[8,4,8192]{2,0,1:T(8,128)S(1)} %copy.5), channel_id=1, replica_groups=mesh['bra'=16,'y'=8,'x'=4,'core'=2] {'x'}, dimensions={1} | all-to-all | bytes 2097152 | tf_op jit(solution)/shard_map/all_to_all | solution.py:40
  84.5 0.1 reduce_sum.18
  84.6 0.2 all_to_all.14
  84.8 18.3 %all_to_all.20 = f32[8,1,8192]{2,1,0:T(1,128)S(1)} all-to-all(f32[8,1,8192]{2,1,0:T(1,128)S(1)} %all_to_all.14), channel_id=1, replica_groups=mesh['bra'=16,'y'=8,'x'=4,'core'=2] {'y'}, dimensions={0} | all-to-all | bytes 524288 | tf_op jit(solution)/shard_map/all_to_all | solution.py:42
  103.1 0.2 reduce_sum.19
  103.3 0.0 copy-done.1
  103.4 0.6 div.3
  (1 shorter events, 0.0 us)
Async XLA Ops:
  0.0 54.7 %copy-start = (f32[3,512,512]{2,1,0:T(8,128)S(1)}, f32[3,512,512]{2,1,0:T(8,128)}, u32[]{:S(2)}) copy-start(f32[3,512,512]{2,1,0:T(8,128)} %param.4) | copy-start | bytes 9437188
  1.8 48.1 %all-to-all-start = ((f32[16,16,512]{2,1,0:T(8,128)}), f32[16,16,512]{2,1,0:T(8,128)}, u32[]{:S(2)}, u32[]{:S(2)}) async-start(f32[16,16,512]{2,1,0:T(8,128)} %broadcast_in_dim.33), calls=%async_computation | async-start | bytes 1048576 | tf_op jit(solution)/shard_map/all_to_all | solution.py:36
  57.9 5.0 %collective-permute-start = (f32[128,2048]{1,0:T(8,128)}, f32[128,2048]{1,0:T(8,128)}, u32[]{:S(2)}, u32[]{:S(2)}) collective-permute-start(f32[128,2048]{1,0:T(8,128)} %pad_maximum_fusion), channel_id=1, source_target_pairs={{0,1},{1,0},{2,3},{3,2},{4,5},{5,4},{6,7},{7,6},{8,9},{9,8},{10,11... | collective-permute-start | bytes 3145736 | tf_op jit(solution)/shard_map/ppermute | solution.py:56
  65.0 38.4 %copy-start.1 = (f32[4,2048]{1,0:T(4,128)S(1)}, f32[4,2048]{1,0:T(4,128)}, u32[]{:S(2)}) copy-start(f32[4,2048]{1,0:T(4,128)} %param.7) | copy-start | bytes 98308

commit v6 on v5

--- a/solution.py
+++ b/solution.py
@@ -32,13 +32,16 @@
 
 def gather_bra(amplitudes):
     n_bra = lax.axis_size("bra")
-    copies = jnp.broadcast_to(amplitudes[None], (n_bra,) + amplitudes.shape)
-    return lax.all_to_all(copies, "bra", 0, 0, tiled=True).reshape(-1, amplitudes.shape[1])
+    rows, width = amplitudes.shape
+    by_core = amplitudes.reshape(2, CORES, rows // (2 * CORES), width)
+    by_core = jnp.transpose(by_core, (1, 0, 2, 3)).reshape(CORES, 1, rows // CORES, width)
+    copies = jnp.broadcast_to(by_core, (CORES, n_bra, rows // CORES, width))
+    return lax.all_to_all(copies, "bra", 1, 1, tiled=True)
 
 
 def reduce_plane(stage):
-    got = lax.all_to_all(stage, "x", 1, 1, tiled=True)
-    stage = jnp.sum(got, axis=1)
+    got = lax.all_to_all(jnp.transpose(stage, (1, 0, 2)), "x", 0, 0, tiled=True)
+    stage = jnp.sum(got, axis=0)
     got = lax.all_to_all(stage, "y", 0, 0, tiled=True)
     return jnp.sum(got, axis=0)
 
@@ -49,9 +52,9 @@
     local_rows = tile_place[:, 0] - lax.axis_index("bra") * row_blocks
     n_y, n_x, n_c = (lax.axis_size(a) for a in KET)
     c = lax.axis_index("core")
-    gathered = gather_bra(amplitudes).reshape(n_y, n_x, n_c, -1, tile_width)
-    own = lax.dynamic_index_in_dim(gathered, c, axis=2, keepdims=False).reshape(-1, tile_width)
-    other = lax.dynamic_index_in_dim(gathered, 1 - c, axis=2, keepdims=False).reshape(-1, tile_width)
+    gathered = gather_bra(amplitudes)
+    own = lax.dynamic_index_in_dim(gathered, c, axis=0, keepdims=False).reshape(-1, tile_width)
+    other = lax.dynamic_index_in_dim(gathered, 1 - c, axis=0, keepdims=False).reshape(-1, tile_width)
     sent = partial_rows(other, integrals, local_rows, row_blocks)
     arrived = lax.ppermute(sent, "core", perm=[(0, 1), (1, 0)])
     stage = partial_rows(own, integrals, local_rows, row_blocks) + arrived

time: 105 us -> 105 us (level)
  matrix products: 4.13 us -> 10.2 us
  local copies, waits for them, and re-layouts: 9.81 us -> 3.89 us
    dot_general x6, matrix products: 4.13 us -> 10.2 us  [tile_term(): lax.dot_general(amp_block, tile_now, (((1,), (1,)), ((), ())), precision=...]
    another operation x1 -> x0, local copies, waits for them, and re-layouts: 1.97 us -> none  [per_device(): gathered = gather_bra(amplitudes).reshape(n_y, n_x, n_c, -1, tile_width)]
    dynamic_slice x1 -> x0, local copies, waits for them, and re-layouts: 1.89 us -> none  [per_device(): lax.dynamic_index_in_dim(gathered, c, axis=2, keepdims=False)]
    reshape x2, local copies, waits for them, and re-layouts: 2.08 us -> 0.94 us  [gather_bra(): by_core = amplitudes.reshape(2, CORES, rows // (2 * CORES), width)]
  transfers between devices with their start and end apart: 2 -> 2, of which waited for: 1 -> 1; matrix products, arithmetic and copies ran while one was open for 4% -> 6% of each run, Pallas kernels for 0% -> 0%
where the time goes in v6:
time: 105 us; the launch traced here: 104 us
  blocking collectives  37.3 us (36%)
  starting transfers between devices  20.8 us (20%)
  waiting for transfers between devices  20.6 us (20%)
  matrix products  10.2 us (10%)
  between operations  7.42 us (7%)
  other arithmetic  4.01 us (4%)
  local copies, waits for them, and re-layouts  3.89 us (4%)
    all_to_all x1, waiting for transfers between devices, gather_bra(): return lax.all_to_all(copies, 'bra', 1, 1, tiled=True)  20.6 us
    all_to_all x1, blocking collectives, reduce_plane(): got = lax.all_to_all(jnp.transpose(stage, (1, 0, 2)), 'x', 0, 0, tiled=True)  18.9 us
    all_to_all x1, starting transfers between devices, gather_bra(): return lax.all_to_all(copies, 'bra', 1, 1, tiled=True)  18.9 us
    all_to_all x1, blocking collectives, reduce_plane(): got = lax.all_to_all(stage, 'y', 0, 0, tiled=True)  18.3 us
    dot_general x6, matrix products, tile_term(): lax.dot_general(amp_block, tile_now, (((1,), (1,)), ((), ())), precision=...  10.2 us
  transfers between devices with their start and end apart: 2, of which 1 were waited for; matrix products, arithmetic and copies ran while one was open for 6% of the time, Pallas kernels for 0%

profile of v6, /device:TPU:2, one launch (start us, length us, event | category | flops | bytes accessed | tf_op | source)
XLA Modules:
  0.0 104.2 jit_solution(8382241167120814259)
XLA Ops:
  0.0 0.0 copy-start
  0.0 0.9 reshape.86
  1.0 0.9 broadcast_in_dim.35
  1.8 18.9 %all-to-all-start = ((f32[2,16,8,512]{3,2,0,1:T(8,128)}), f32[2,16,8,512]{3,2,0,1:T(8,128)}, u32[]{:S(2)}, u32[]{:S(2)}) async-start(f32[2,16,8,512]{3,2,0,1:T(8,128)} %broadcast_in_dim.35), calls=%async_computation | async-start | bytes 1048576 | tf_op jit(solution)/shard_map/all_to_all | solution.py:39
  20.7 0.7 slice_subtract_fusion
  21.4 0.6 fusion.36
  29.3 20.6 %all-to-all-done = f32[2,16,8,512]{3,2,0,1:T(8,128)} async-done(((f32[2,16,8,512]{3,2,0,1:T(8,128)}), f32[2,16,8,512]{3,2,0,1:T(8,128)}, u32[]{:S(2)}, u32[]{:S(2)}) %all-to-all-start) | async-done | bytes 524320 | tf_op jit(solution)/shard_map/all_to_all | solution.py:39
  49.9 2.0 %fusion.8 = f32[128,512]{1,0:T(8,128)S(1)} fusion(f32[3,512,512]{2,1,0:T(8,128)} %param.4, f32[2,16,8,512]{3,2,0,1:T(8,128)} %all-to-all-done, s32[]{:T(128)S(6)} %select_n.154), kind=kOutput, calls=%fused_computation.10 | convolution fusion | flops 201326592 | bytes 1572868 | tf_op jit(solution)/shard_map/dot_general | solution.py:13
  51.9 0.0 copy-done
  51.9 1.6 %fusion.4 = f32[128,512]{1,0:T(8,128)S(1)} fusion(f32[3,512,512]{2,1,0:T(8,128)S(1)} %copy-done, f32[2,16,8,512]{3,2,0,1:T(8,128)} %all-to-all-done, s32[]{:T(128)S(6)} %select_n.154), kind=kOutput, calls=%fused_computation.6 | convolution fusion | flops 201326592 | bytes 1572868 | tf_op jit(solution)/shard_map/dot_general | solution.py:13
  53.5 1.7 %select_add_fusion.3 = (f32[128,512]{1,0:T(8,128)S(1)}, f32[128,512]{1,0:T(8,128)S(1)}, f32[128,512]{1,0:T(8,128)S(1)}, f32[128,512]{1,0:T(8,128)S(1)}) fusion(f32[128,512]{1,0:T(8,128)S(1)} %fusion.4, f32[128,512]{1,0:T(8,128)S(1)} %fusion.8, pred[]{:T(512)} %bitcast.7, pred[]{:T(512)} %bitcast.5, pred[]{:T(512)} %bitcast, pred[]{:T(512)} %bitcast.17, ...), kind=kOutput, calls=%fused_computation.30 | convolution fusion | flops 202637312 | bytes 2889732 | tf_op jit(solution)/shard_map/dot_general | solution.py:13
  55.2 1.0 %pad_maximum_fusion = f32[128,2048]{1,0:T(8,128)} fusion(f32[128,512]{1,0:T(8,128)S(1)} %get-tuple-element.10, f32[128,512]{1,0:T(8,128)S(1)} %get-tuple-element.11, f32[128,512]{1,0:T(8,128)S(1)} %get-tuple-element.12, f32[128,512]{1,0:T(8,128)S(1)} %get-tuple-element.9), kind=kLoop, calls=%fused_computation.1 | loop fusion | flops 786432 | bytes 2097152 | tf_op jit(solution)/shard_map/concatenate | solution.py:30
  56.3 1.9 %collective-permute-start = (f32[128,2048]{1,0:T(8,128)}, f32[128,2048]{1,0:T(8,128)}, u32[]{:S(2)}, u32[]{:S(2)}) collective-permute-start(f32[128,2048]{1,0:T(8,128)} %pad_maximum_fusion), channel_id=1, source_target_pairs={{0,1},{1,0},{2,3},{3,2},{4,5},{5,4},{6,7},{7,6},{8,9},{9,8},{10,11... | collective-permute-start | bytes 3145736 | tf_op jit(solution)/shard_map/ppermute | solution.py:59
  58.2 1.6 %fusion.10 = f32[128,512]{1,0:T(8,128)S(1)} fusion(f32[3,512,512]{2,1,0:T(8,128)S(1)} %copy-done, f32[2,16,8,512]{3,2,0,1:T(8,128)} %all-to-all-done, s32[]{:T(128)S(6)} %select_n.130), kind=kOutput, calls=%fused_computation.12 | convolution fusion | flops 201326592 | bytes 1572868 | tf_op jit(solution)/shard_map/dot_general | solution.py:13
  59.8 1.6 %fusion.6 = f32[128,512]{1,0:T(8,128)S(1)} fusion(f32[3,512,512]{2,1,0:T(8,128)S(1)} %copy-done, f32[2,16,8,512]{3,2,0,1:T(8,128)} %all-to-all-done, s32[]{:T(128)S(6)} %select_n.130), kind=kOutput, calls=%fused_computation.8 | convolution fusion | flops 201326592 | bytes 1572868 | tf_op jit(solution)/shard_map/dot_general | solution.py:13
  61.4 1.7 %select_add_fusion.7 = (f32[128,512]{1,0:T(8,128)S(1)}, f32[128,512]{1,0:T(8,128)S(1)}, f32[128,512]{1,0:T(8,128)S(1)}, f32[128,512]{1,0:T(8,128)S(1)}) fusion(f32[128,512]{1,0:T(8,128)S(1)} %fusion.6, f32[128,512]{1,0:T(8,128)S(1)} %fusion.10, pred[]{:T(512)} %bitcast.7, pred[]{:T(512)} %bitcast.5, pred[]{:T(512)} %bitcast, pred[]{:T(512)} %bitcast.17, ...), kind=kOutput, calls=%fused_computation.34 | convolution fusion | flops 202637312 | bytes 2889732 | tf_op jit(solution)/shard_map/dot_general | solution.py:13
  63.1 0.0 collective-permute-done
  63.2 1.4 %maximum_add_fusion = f32[128,2048]{1,0:T(8,128)S(1)} fusion(f32[128,2048]{1,0:T(8,128)} %collective-permute-done, f32[128,512]{1,0:T(8,128)S(1)} %get-tuple-element.6, f32[128,512]{1,0:T(8,128)S(1)} %get-tuple-element.7, f32[128,512]{1,0:T(8,128)S(1)} %get-tuple-element.8, f32[128,512]{1,0:T(8,128)S(1)} %get-tuple-element.5), kind=kLoop, calls=%fused_computation | loop fusion | flops 1048576 | bytes 3145728 | tf_op jit(solution)/shard_map/add | solution.py:60
  64.5 0.6 reshape.89
  65.2 0.0 copy-start.1
  65.2 0.6 copy.11
  65.8 18.9 %all_to_all.19 = f32[4,8,8192]{2,1,0:T(8,128)S(1)} all-to-all(f32[4,8,8192]{2,1,0:T(8,128)S(1)} %bitcast.55), channel_id=1, replica_groups=mesh['bra'=16,'y'=8,'x'=4,'core'=2] {'x'}, dimensions={0} | all-to-all | bytes 2097152 | tf_op jit(solution)/shard_map/all_to_all | solution.py:43
  84.7 0.1 reduce_sum.18
  84.8 0.2 all_to_all.14
  85.0 18.3 %all_to_all.20 = f32[8,1,8192]{2,1,0:T(1,128)S(1)} all-to-all(f32[8,1,8192]{2,1,0:T(1,128)S(1)} %all_to_all.14), channel_id=1, replica_groups=mesh['bra'=16,'y'=8,'x'=4,'core'=2] {'y'}, dimensions={0} | all-to-all | bytes 524288 | tf_op jit(solution)/shard_map/all_to_all | solution.py:45
  103.4 0.2 reduce_sum.19
  103.6 0.0 copy-done.1
  103.6 0.6 div.3
  (3 shorter events, 0.0 us)
Async XLA Ops:
  0.0 51.9 %copy-start = (f32[3,512,512]{2,1,0:T(8,128)S(1)}, f32[3,512,512]{2,1,0:T(8,128)}, u32[]{:S(2)}) copy-start(f32[3,512,512]{2,1,0:T(8,128)} %param.4) | copy-start | bytes 9437188
  1.8 48.1 %all-to-all-start = ((f32[2,16,8,512]{3,2,0,1:T(8,128)}), f32[2,16,8,512]{3,2,0,1:T(8,128)}, u32[]{:S(2)}, u32[]{:S(2)}) async-start(f32[2,16,8,512]{3,2,0,1:T(8,128)} %broadcast_in_dim.35), calls=%async_computation | async-start | bytes 1048576 | tf_op jit(solution)/shard_map/all_to_all | solution.py:39
  56.3 6.9 %collective-permute-start = (f32[128,2048]{1,0:T(8,128)}, f32[128,2048]{1,0:T(8,128)}, u32[]{:S(2)}, u32[]{:S(2)}) collective-permute-start(f32[128,2048]{1,0:T(8,128)} %pad_maximum_fusion), channel_id=1, source_target_pairs={{0,1},{1,0},{2,3},{3,2},{4,5},{5,4},{6,7},{7,6},{8,9},{9,8},{10,11... | collective-permute-start | bytes 3145736 | tf_op jit(solution)/shard_map/ppermute | solution.py:59
  65.2 38.4 %copy-start.1 = (f32[4,2048]{1,0:T(4,128)S(1)}, f32[4,2048]{1,0:T(4,128)}, u32[]{:S(2)}) copy-start(f32[4,2048]{1,0:T(4,128)} %param.7) | copy-start | bytes 98308

commit v7 on v5

--- a/solution.py
+++ b/solution.py
@@ -37,8 +37,8 @@
 
 
 def reduce_plane(stage):
-    got = lax.all_to_all(stage, "x", 1, 1, tiled=True)
-    stage = jnp.sum(got, axis=1)
+    got = lax.all_to_all(jnp.transpose(stage, (1, 0, 2)), "x", 0, 0, tiled=True)
+    stage = jnp.sum(got, axis=0)
     got = lax.all_to_all(stage, "y", 0, 0, tiled=True)
     return jnp.sum(got, axis=0)
 

time: 105 us -> 105 us (level)
  no operation moved by 1% of the time
where the time goes in v7:
time: 105 us; the launch traced here: 104 us
  blocking collectives  37.3 us (36%)
  starting transfers between devices  20.8 us (20%)
  waiting for transfers between devices  20.2 us (19%)
  local copies, waits for them, and re-layouts  9.81 us (9%)
  between operations  7.75 us (7%)
  matrix products  4.13 us (4%)
  other arithmetic  4 us (4%)
    all_to_all x1, waiting for transfers between devices, gather_bra(): lax.all_to_all(copies, 'bra', 0, 0, tiled=True)  20.2 us
    all_to_all x1, blocking collectives, reduce_plane(): got = lax.all_to_all(jnp.transpose(stage, (1, 0, 2)), 'x', 0, 0, tiled=True)  18.9 us
    all_to_all x1, starting transfers between devices, gather_bra(): lax.all_to_all(copies, 'bra', 0, 0, tiled=True)  18.9 us
    all_to_all x1, blocking collectives, reduce_plane(): got = lax.all_to_all(stage, 'y', 0, 0, tiled=True)  18.3 us
    dot_general x6, matrix products, tile_term(): lax.dot_general(amp_block, tile_now, (((1,), (1,)), ((), ())), precision=...  4.13 us
  transfers between devices with their start and end apart: 2, of which 1 were waited for; matrix products, arithmetic and copies ran while one was open for 4% of the time, Pallas kernels for 0%

profile of v7, /device:TPU:2, one launch (start us, length us, event | category | flops | bytes accessed | tf_op | source)
XLA Modules:
  0.0 104.0 jit_solution(6170884317646899793)
XLA Ops:
  0.0 0.0 copy-start
  0.0 1.7 %broadcast_in_dim.33 = f32[16,16,512]{2,1,0:T(8,128)} broadcast(f32[16,512]{1,0:T(8,128)} %param.6), dimensions={1,2} | broadcast | bytes 557056 | tf_op jit(solution)/shard_map/broadcast_in_dim | solution.py:35
  1.8 18.9 %all-to-all-start = ((f32[16,16,512]{2,1,0:T(8,128)}), f32[16,16,512]{2,1,0:T(8,128)}, u32[]{:S(2)}, u32[]{:S(2)}) async-start(f32[16,16,512]{2,1,0:T(8,128)} %broadcast_in_dim.33), calls=%async_computation | async-start | bytes 1048576 | tf_op jit(solution)/shard_map/all_to_all | solution.py:36
  20.7 0.7 slice_subtract_fusion
  21.4 0.7 fusion.18
  29.6 20.2 %all-to-all-done = f32[16,16,512]{2,1,0:T(8,128)} async-done(((f32[16,16,512]{2,1,0:T(8,128)}), f32[16,16,512]{2,1,0:T(8,128)}, u32[]{:S(2)}, u32[]{:S(2)}) %all-to-all-start) | async-done | bytes 524320 | tf_op jit(solution)/shard_map/all_to_all | solution.py:36
  49.8 2.0 %reshape_reshape.3 = f32[8,4,2,4,512]{4,3,2,1,0:T(4,128)} reshape(f32[16,16,512]{2,1,0:T(8,128)} %all-to-all-done) | data formatting | bytes 1048576 | tf_op jit(solution)/shard_map/reshape;reshape | solution.py:52
  51.8 1.9 %constant_dynamic-slice_fusion.1 = (f32[8,4,1,4,512]{4,3,2,1,0:T(4,128)}, f32[8,4,1,4,512]{4,3,2,1,0:T(4,128)}) fusion(f32[8,4,2,4,512]{4,3,2,1,0:T(4,128)} %reshape_reshape.3, s32[]{:T(128)S(6)} %select_n.130, s32[]{:T(128)S(6)} %select_n.154), kind=kLoop, calls=%fused_computation.30 | loop fusion | bytes 1048584 | tf_op jit(solution)/shard_map/jit(dynamic_index_in_dim)/dynamic_slice | solution.py:53
  53.7 1.0 %reshape.83 = f32[128,512]{1,0:T(8,128)S(1)} reshape(f32[8,4,1,4,512]{4,3,2,1,0:T(4,128)} %get-tuple-element.14) | data formatting | bytes 524288 | tf_op jit(solution)/shard_map/reshape | solution.py:54
  54.7 0.0 copy-done
  54.7 0.7 fusion.4
  55.4 0.7 fusion.8
  56.1 0.7 select_add_fusion.3
  56.8 1.0 %pad_maximum_fusion = f32[128,2048]{1,0:T(8,128)} fusion(f32[128,512]{1,0:T(8,128)S(1)} %get-tuple-element.10, f32[128,512]{1,0:T(8,128)S(1)} %get-tuple-element.11, f32[128,512]{1,0:T(8,128)S(1)} %get-tuple-element.12, f32[128,512]{1,0:T(8,128)S(1)} %get-tuple-element.9), kind=kLoop, calls=%fused_computation.1 | loop fusion | flops 786432 | bytes 2097152 | tf_op jit(solution)/shard_map/concatenate | solution.py:30
  57.9 1.9 %collective-permute-start = (f32[128,2048]{1,0:T(8,128)}, f32[128,2048]{1,0:T(8,128)}, u32[]{:S(2)}, u32[]{:S(2)}) collective-permute-start(f32[128,2048]{1,0:T(8,128)} %pad_maximum_fusion), channel_id=1, source_target_pairs={{0,1},{1,0},{2,3},{3,2},{4,5},{5,4},{6,7},{7,6},{8,9},{9,8},{10,11... | collective-permute-start | bytes 3145736 | tf_op jit(solution)/shard_map/ppermute | solution.py:56
  59.8 1.0 %reshape.82 = f32[128,512]{1,0:T(8,128)S(1)} reshape(f32[8,4,1,4,512]{4,3,2,1,0:T(4,128)} %get-tuple-element.13) | data formatting | bytes 524288 | tf_op jit(solution)/shard_map/reshape | solution.py:53
  60.8 0.7 fusion.6
  61.5 0.7 fusion.10
  62.2 0.7 select_add_fusion.7
  62.9 0.0 collective-permute-done
  62.9 1.4 %maximum_add_fusion = f32[128,2048]{1,0:T(8,128)S(1)} fusion(f32[128,2048]{1,0:T(8,128)} %collective-permute-done, f32[128,512]{1,0:T(8,128)S(1)} %get-tuple-element.6, f32[128,512]{1,0:T(8,128)S(1)} %get-tuple-element.7, f32[128,512]{1,0:T(8,128)S(1)} %get-tuple-element.8, f32[128,512]{1,0:T(8,128)S(1)} %get-tuple-element.5), kind=kLoop, calls=%fused_computation | loop fusion | flops 1048576 | bytes 3145728 | tf_op jit(solution)/shard_map/add | solution.py:57
  64.3 0.6 reshape.84
  65.0 0.0 copy-start.1
  65.0 0.6 copy.7
  65.6 18.9 %all_to_all.19 = f32[4,8,8192]{2,1,0:T(8,128)S(1)} all-to-all(f32[4,8,8192]{2,1,0:T(8,128)S(1)} %bitcast.40), channel_id=1, replica_groups=mesh['bra'=16,'y'=8,'x'=4,'core'=2] {'x'}, dimensions={0} | all-to-all | bytes 2097152 | tf_op jit(solution)/shard_map/all_to_all | solution.py:40
  84.5 0.1 reduce_sum.18
  84.6 0.2 all_to_all.14
  84.8 18.3 %all_to_all.20 = f32[8,1,8192]{2,1,0:T(1,128)S(1)} all-to-all(f32[8,1,8192]{2,1,0:T(1,128)S(1)} %all_to_all.14), channel_id=1, replica_groups=mesh['bra'=16,'y'=8,'x'=4,'core'=2] {'y'}, dimensions={0} | all-to-all | bytes 524288 | tf_op jit(solution)/shard_map/all_to_all | solution.py:42
  103.1 0.2 reduce_sum.19
  103.3 0.0 copy-done.1
  103.4 0.6 div.3
  (1 shorter events, 0.0 us)
Async XLA Ops:
  0.0 54.7 %copy-start = (f32[3,512,512]{2,1,0:T(8,128)S(1)}, f32[3,512,512]{2,1,0:T(8,128)}, u32[]{:S(2)}) copy-start(f32[3,512,512]{2,1,0:T(8,128)} %param.4) | copy-start | bytes 9437188
  1.8 48.1 %all-to-all-start = ((f32[16,16,512]{2,1,0:T(8,128)}), f32[16,16,512]{2,1,0:T(8,128)}, u32[]{:S(2)}, u32[]{:S(2)}) async-start(f32[16,16,512]{2,1,0:T(8,128)} %broadcast_in_dim.33), calls=%async_computation | async-start | bytes 1048576 | tf_op jit(solution)/shard_map/all_to_all | solution.py:36
  57.9 5.0 %collective-permute-start = (f32[128,2048]{1,0:T(8,128)}, f32[128,2048]{1,0:T(8,128)}, u32[]{:S(2)}, u32[]{:S(2)}) collective-permute-start(f32[128,2048]{1,0:T(8,128)} %pad_maximum_fusion), channel_id=1, source_target_pairs={{0,1},{1,0},{2,3},{3,2},{4,5},{5,4},{6,7},{7,6},{8,9},{9,8},{10,11... | collective-permute-start | bytes 3145736 | tf_op jit(solution)/shard_map/ppermute | solution.py:56
  65.0 38.4 %copy-start.1 = (f32[4,2048]{1,0:T(4,128)S(1)}, f32[4,2048]{1,0:T(4,128)}, u32[]{:S(2)}) copy-start(f32[4,2048]{1,0:T(4,128)} %param.7) | copy-start | bytes 98308
